TPU v7x, 256 devices: a whole 4x4x8 slice. The times are simulated.
256 devices in a mesh: batch: 8 (over z), replica: 32 (over y, x, core).
Axes of the slice: x: 4, y: 4, z: 8, core: 2. Of those that a mesh axis runs over, the one named last changes fastest.
Arguments:
- patches: bfloat16 [32, 64, 64, 1024], P('replica', 'batch'), may hold values from -6 to 6
- visible_order: int32 [32, 64, 64], P('replica', 'batch'), may hold values from 0 to 63, each once within a row
- visible_counts: int32 [32, 64], P('replica'), may hold values from 1 to 32, as said below
- dest_rows: int32 [32, 64], P('replica'), may hold values from 0 to 1023, as said below
- qkv_weight: bfloat16 [1024, 3072], P('replica')
- out_weight: bfloat16 [1024, 1024], P('replica'), may hold values from -0.1875 to 0.1875
- norm_gain: bfloat16 [1024], P('replica'), may hold values from 0.5 to 1.5
- upstream: bfloat16 [32, 1024, 1024], P('replica', 'batch'), may hold values from -6 to 6
Outputs:
- layer_out: bfloat16 [32, 1024, 1024], P('replica', 'batch')
- d_packed: bfloat16 [32, 1024, 1024], P('replica', 'batch')
- grad_qkv: float32 [1024, 3072], P('replica')
- grad_out: float32 [1024, 1024], P('replica')
- grad_gain: float32 [1024], P('replica')
Inputs may be any that keep to these rules, and one draw needn't show every extreme that they name: `visible_counts`: in every replica index, each batch index b packs exactly 128 rows: the volumes with dest_rows // 128 == b, one from every device of the batch axis, in order of that device's batch index, without gaps; one of them has 32 visible patches. `dest_rows`: the 8 volumes of one device go to 8 different batch indices; a volume's rows never cross a multiple of 128.
All inputs are finite; a program needn't handle non-finite values.
Results may differ from a plain program's by a relative error of at most 0.033.
Values may be sent and summed in bfloat16 or wider, within the bound.
No kernel may reach another device: no remote copies, remote signals or barrier semaphores. Data moves between devices by JAX's collectives and lax.ppermute only.
A program may use at most 128 MiB of HBM per device.

v0:
```python
import jax
import jax.numpy as jnp
from jax import lax
from jax.sharding import PartitionSpec as P

HEADS = 16
MAXVIS = 32
MEANVIS = 16
EPS = 1e-06
NEG = -1e30


def layer_core(tokens, upward, allowed, wqkv, wout, gain):
    groups, length, width = tokens.shape
    rows = groups * length
    head_dim = width // HEADS
    scale = head_dim ** (-0.5)
    x32 = tokens.astype(jnp.float32).reshape(rows, width)
    row_average = jnp.mean(x32, axis=1, keepdims=True)
    centered_rows = x32 - row_average
    inverse_deviation = lax.rsqrt(
        jnp.mean(centered_rows * centered_rows, axis=1, keepdims=True) + EPS
    )
    standardized_rows = centered_rows * inverse_deviation
    gain_float32 = gain.astype(jnp.float32)
    layernorm_output = (standardized_rows * gain_float32).astype(jnp.bfloat16)
    qkv = jnp.dot(layernorm_output, wqkv, preferred_element_type=jnp.float32).astype(jnp.bfloat16)
    query = qkv[:, :width].reshape(groups, length, HEADS, head_dim)
    keys = qkv[:, width : 2 * width].reshape(groups, length, HEADS, head_dim)
    values = qkv[:, 2 * width :].reshape(groups, length, HEADS, head_dim)
    scores = jnp.einsum("gqhd,gkhd->ghqk", query, keys, preferred_element_type=jnp.float32) * scale
    scores = jnp.where(allowed[:, None], scores, NEG)
    top = jnp.max(scores, axis=-1, keepdims=True)
    expd = jnp.exp(scores - top)
    probs = expd / jnp.sum(expd, axis=-1, keepdims=True)
    weights = probs.astype(jnp.bfloat16)
    context = (
        jnp.einsum("ghqk,gkhd->gqhd", weights, values, preferred_element_type=jnp.float32)
        .astype(jnp.bfloat16)
        .reshape(rows, width)
    )
    result = (x32 + jnp.dot(context, wout, preferred_element_type=jnp.float32)).astype(jnp.bfloat16)
    up_rows = upward.reshape(rows, width)
    d_context = lax.dot_general(
        up_rows, wout, (((1,), (1,)), ((), ())), preferred_element_type=jnp.float32
    ).astype(jnp.bfloat16)
    d_context = d_context.reshape(groups, length, HEADS, head_dim)
    d_values = jnp.einsum(
        "ghqk,gqhd->gkhd", weights, d_context, preferred_element_type=jnp.float32
    ).astype(jnp.bfloat16)
    d_weights = jnp.einsum("gqhd,gkhd->ghqk", d_context, values, preferred_element_type=jnp.float32)
    d_scores = (
        probs * (d_weights - jnp.sum(d_weights * probs, axis=-1, keepdims=True)) * scale
    ).astype(jnp.bfloat16)
    d_query = jnp.einsum(
        "ghqk,gkhd->gqhd", d_scores, keys, preferred_element_type=jnp.float32
    ).astype(jnp.bfloat16)
    d_keys = jnp.einsum(
        "ghqk,gqhd->gkhd", d_scores, query, preferred_element_type=jnp.float32
    ).astype(jnp.bfloat16)
    d_qkv = jnp.concatenate(
        [d_query.reshape(rows, width), d_keys.reshape(rows, width), d_values.reshape(rows, width)],
        axis=1,
    )
    layernorm_gradient = lax.dot_general(
        d_qkv, wqkv, (((1,), (1,)), ((), ())), preferred_element_type=jnp.float32
    )
    gain_products = jnp.sum(layernorm_gradient * standardized_rows, axis=0)
    normalized_gradient = layernorm_gradient * gain_float32
    input_gradient = inverse_deviation * (
        normalized_gradient
        - jnp.mean(normalized_gradient, axis=1, keepdims=True)
        - standardized_rows
        * jnp.mean(normalized_gradient * standardized_rows, axis=1, keepdims=True)
    )
    d_tokens = (up_rows.astype(jnp.float32) + input_gradient).astype(jnp.bfloat16)
    return (
        result.reshape(tokens.shape),
        d_tokens.reshape(tokens.shape),
        layernorm_output,
        context,
        d_qkv,
        up_rows,
        gain_products,
    )


def left_product(left, right):
    return lax.dot_general(
        left, right, (((0,), (0,)), ((), ())), preferred_element_type=jnp.float32
    )


def on_device(
    patches, visible_order, visible_counts, dest_rows, qkv_weight, out_weight, norm_gain, upstream
):
    qkv_cols = qkv_weight.shape[1]
    out_cols = out_weight.shape[1]
    gain_block = jnp.broadcast_to(norm_gain[:, None], (norm_gain.shape[0], 128))
    gathered = lax.all_gather(
        jnp.concatenate([qkv_weight, out_weight, gain_block], axis=1), "replica", axis=0, tiled=True
    )
    wqkv = gathered[:, :qkv_cols]
    wout = gathered[:, qkv_cols : qkv_cols + out_cols]
    gain = gathered[:, qkv_cols + out_cols]
    batches = lax.axis_size("batch")
    me_index = lax.axis_index("batch")
    cap = MEANVIS * batches
    width = wout.shape[1]
    slot = jnp.arange(MAXVIS, dtype=jnp.int32)
    sources = jnp.arange(batches, dtype=jnp.int32)
    counts_all = visible_counts[0].reshape(batches, batches)
    rows_all = dest_rows[0].reshape(batches, batches)
    mine = rows_all // cap == me_index
    src_count = jnp.sum(jnp.where(mine, counts_all, 0), axis=1)
    src_start = jnp.sum(jnp.where(mine, rows_all % cap, 0), axis=1)
    position = jnp.arange(cap, dtype=jnp.int32)
    hit = (position[:, None] >= src_start[None, :]) & (
        position[:, None] < (src_start + src_count)[None, :]
    )
    segment = jnp.sum(jnp.where(hit, sources[None, :], 0), axis=1)
    inside = jnp.sum(jnp.where(hit, position[:, None] - src_start[None, :], 0), axis=1)
    flat_rows = segment * MAXVIS + inside
    my_targets = jnp.take(rows_all, me_index, axis=0) // cap
    to_target = jnp.sum(
        jnp.where(my_targets[None, :] == sources[:, None], sources[None, :], 0), axis=1
    )
    my_counts = jnp.take(counts_all, me_index, axis=0)
    local_rows = jnp.take_along_axis(patches[0], visible_order[0, :, :MAXVIS, None], axis=1)
    live = slot[None, :] < src_count[:, None]
    pick = jnp.clip(src_start[:, None] + slot[None, :], 0, cap - 1)
    fetched = jnp.take(upstream[0], pick.reshape(-1), axis=0).reshape(batches, MAXVIS, width)
    backward_rows = jnp.where(live[..., None], fetched, jnp.zeros_like(fetched))
    returned = lax.all_to_all(backward_rows, "batch", split_axis=0, concat_axis=0, tiled=True)
    upward = jnp.take(returned, my_targets, axis=0)
    valid = slot[None, :] < my_counts[:, None]
    allowed = jnp.broadcast_to(valid[:, None, :], (batches, MAXVIS, MAXVIS))
    result, d_tokens, layernorm_output, context, d_qkv, up_rows, gain_products = layer_core(
        local_rows, upward, allowed, wqkv, wout, gain
    )
    came = lax.all_to_all(
        jnp.take(jnp.concatenate([result, d_tokens], axis=-1), to_target, axis=0),
        "batch",
        split_axis=0,
        concat_axis=0,
        tiled=True,
    )
    came_out = came[..., :width]
    came_grad = came[..., width:]
    layer_out = jnp.take(came_out.reshape(batches * MAXVIS, width), flat_rows, axis=0)
    d_packed = jnp.take(came_grad.reshape(batches * MAXVIS, width), flat_rows, axis=0)
    partial = jnp.concatenate(
        [
            left_product(layernorm_output, d_qkv).astype(jnp.bfloat16),
            left_product(context, up_rows).astype(jnp.bfloat16),
            jnp.broadcast_to(gain_products.astype(jnp.bfloat16)[:, None], (width, 128)),
        ],
        axis=1,
    )
    summed = lax.psum_scatter(partial, "replica", scatter_dimension=0, tiled=True)
    summed = lax.psum(summed, "batch").astype(jnp.float32)
    grad_q = summed[:, :qkv_cols]
    grad_o = summed[:, qkv_cols : qkv_cols + out_cols]
    grad_g = summed[:, qkv_cols + out_cols]
    return (layer_out[None], d_packed[None], grad_q, grad_o, grad_g)


def solution(mesh):
    placed = (
        P("replica", "batch", None, None),
        P("replica", "batch", None),
        P("replica", None),
        P("replica", None),
        P("replica", None),
        P("replica", None),
        P("replica"),
        P("replica", "batch", None),
    )
    return jax.shard_map(
        on_device,
        mesh=mesh,
        in_specs=placed,
        out_specs=(
            P("replica", "batch", None),
            P("replica", "batch", None),
            P("replica", None),
            P("replica", None),
            P("replica"),
        ),
        check_vma=False,
    )
```

profile of v0, /device:TPU:2, one launch (start us, length us, event | category | flops | bytes accessed | tf_op | source)
XLA Modules:
  0.0 334.6 jit_solution(9900112664250814567)
XLA Ops:
  15.7 8.5 %all-to-all-start = ((bf16[8,32,1024]{2,1,0:T(8,128)(2,1)}), bf16[8,32,1024]{2,1,0:T(8,128)(2,1)S(1)}, u32[]{:S(2)}, u32[]{:S(2)}) async-start(bf16[8,32,1024]{2,1,0:T(8,128)(2,1)} %select_select_fusion), calls=%async_computation | async-start | bytes 1048576 | tf_op jit(solution)/shard_map/all_to_all | solution.py:134
  24.3 2.8 gather_fusion.3
  28.2 13.4 %all-to-all-done = bf16[8,32,1024]{2,1,0:T(8,128)(2,1)S(1)} async-done(((bf16[8,32,1024]{2,1,0:T(8,128)(2,1)}), bf16[8,32,1024]{2,1,0:T(8,128)(2,1)S(1)}, u32[]{:S(2)}, u32[]{:S(2)}) %all-to-all-start) | async-done | bytes 524320 | tf_op jit(solution)/shard_map/all_to_all | solution.py:134
  43.3 29.1 %all-gather.2.cloned.1.call-done = bf16[1024,4224]{1,0:T(8,128)(2,1)} async-done(((bf16[32,4224]{1,0:T(8,128)(2,1)}), bf16[1024,4224]{1,0:T(8,128)(2,1)}) %all-gather.2.cloned.1.call-update) | async-done | bytes 8650768 | tf_op jit(solution)/shard_map/all_gather | solution.py:100
  72.4 3.2 fusion.43
  78.4 4.7 %fusion.6 = bf16[256,3072]{1,0:T(8,128)(2,1)S(1)} fusion(bf16[1024,4224]{1,0:T(8,128)(2,1)} %all-gather.2.cloned.1.call-done, f32[1024]{0:T(1024)S(1)} %convert_reduce_fusion.1, f32[256]{0:T(256)S(1)} %rsqrt.12, f32[256]{0:T(256)S(1)} %div.51, bf16[256,1024]{1,0:T(8,128)(2,1)S(1)} %gather_fusion.3, pred[256]{0:T(512)(128)(4,1)S(1)} %compare_and_fusion.4), kind=kOutput, calls=%fused_computation.14 | convolution fusion | flops 1612972032 | bytes 8395008 | tf_op jit(solution)/shard_map/dot_general | solution.py:27
  84.4 2.5 reshape.302
  86.9 2.5 reshape.304
  89.4 2.5 reshape.303
  91.9 3.2 fusion.66
  95.1 4.1 %fusion.111 = (f32[8,16,32]{2,1,0:T(8,128)S(1)}, f32[8,16,32,32]{2,3,1,0:T(8,128)}) fusion(pred[8,32]{1,0:T(8,128)(4,1)S(1)} %iota_compare_fusion.3, bf16[8,32,16,64]{3,2,1,0:T(8,128)(2,1)} %reshape.304, bf16[8,32,16,64]{3,2,1,0:T(8,128)(2,1)} %reshape.303), kind=kOutput, calls=%fused_computation.155 | convolution fusion | flops 17301536 | bytes 1589504 | tf_op jit(solution)/shard_map/sub | solution.py:34
  99.2 5.8 %fusion.34 = bf16[8,32,16,64]{3,1,2,0:T(8,128)(2,1)} fusion(f32[8,16,32,32]{2,3,1,0:T(8,128)} %fusion.66, bf16[8,32,16,64]{3,2,1,0:T(8,128)(2,1)} %reshape.304, f32[8,16,32,32]{2,3,1,0:T(8,128)} %get-tuple-element.37, f32[8,16,32]{2,1,0:T(8,128)S(1)} %get-tuple-element.36), kind=kOutput, calls=%fused_computation.35 | convolution fusion | flops 17960992 | bytes 2113536 | tf_op jit(solution)/shard_map/ghqk,gkhd->gqhd/dot_general | solution.py:55
  104.9 5.6 %fusion.31 = bf16[8,32,16,64]{3,1,2,0:T(8,128)(2,1)} fusion(f32[8,16,32,32]{2,3,1,0:T(8,128)} %fusion.66, bf16[8,32,16,64]{3,2,1,0:T(8,128)(2,1)} %reshape.303, f32[8,16,32,32]{2,3,1,0:T(8,128)} %get-tuple-element.37, f32[8,16,32]{2,1,0:T(8,128)S(1)} %get-tuple-element.36), kind=kOutput, calls=%fused_computation.34 | convolution fusion | flops 17960992 | bytes 2113536 | tf_op jit(solution)/shard_map/ghqk,gqhd->gkhd/dot_general | solution.py:58
  110.6 3.2 fusion.30
  117.3 1.9 constant_dynamic-update-slice_fusion.2
  128.7 1.9 constant_dynamic-update-slice_fusion.1
  130.7 1.9 constant_dynamic-update-slice_fusion
  132.6 3.5 %convolution_convert_fusion = bf16[1024,3072]{1,0:T(8,128)(2,1)S(1)} fusion(bf16[256,3072]{1,0:T(8,128)(2,1)} %constant_dynamic-update-slice_fusion, f32[1024]{0:T(1024)S(1)} %convert_reduce_fusion.1, f32[256]{0:T(256)S(1)} %rsqrt.12, f32[256]{0:T(256)S(1)} %div.51, bf16[256,1024]{1,0:T(8,128)(2,1)S(1)} %gather_fusion.3, pred[256]{0:T(512)(128)(4,1)S(1)} %compare_and_fusion.4), kind=kOutput, calls=%fused_computation.9 | convolution fusion | flops 1615331328 | bytes 8395008 | tf_op jit(solution)/shard_map/dot_general | solution.py:89
  137.5 5.8 %fusion.57 = (bf16[1024]{0:T(1024)(128)(2,1)S(1)}, f32[256]{0:T(256)S(1)}, f32[256]{0:T(256)S(1)}, f32[256,1024]{1,0:T(8,128)}) fusion(f32[256]{0:T(256)S(1)} %rsqrt.12, f32[256]{0:T(256)S(1)} %div.51, bf16[256,1024]{1,0:T(8,128)(2,1)S(1)} %gather_fusion.3, pred[256]{0:T(512)(128)(4,1)S(1)} %compare_and_fusion.4, f32[1024]{0:T(1024)S(1)} %convert_reduce_fusion.1, ...), kind=kOutput, calls=%fused_computation.53 | convolution fusion | flops 1613232640 | bytes 9447680 | tf_op jit(solution)/shard_map/dot_general | solution.py:65
  143.5 3.7 %pad_maximum_fusion = bf16[1024,4224]{1,0:T(8,128)(2,1)} fusion(bf16[1024,128]{1,0:T(8,128)(2,1)S(1)} %broadcast_in_dim.181, bf16[1024,1024]{1,0:T(8,128)(2,1)S(1)} %convolution_convert_fusion.1, bf16[1024,3072]{1,0:T(8,128)(2,1)S(1)} %convolution_convert_fusion), kind=kLoop, calls=%fused_computation.8 | loop fusion | flops 25952256 | bytes 17301504 | tf_op jit(solution)/shard_map/concatenate | solution.py:152
  149.2 2.3 fusion.40
  153.4 7.0 %all-to-all-start.1 = ((bf16[8,32,2048]{2,1,0:T(8,128)(2,1)}), bf16[8,32,2048]{2,1,0:T(8,128)(2,1)S(1)}, u32[]{:S(2)}, u32[]{:S(2)}) async-start(bf16[8,32,2048]{2,1,0:T(8,128)(2,1)} %broadcast_select_fusion), calls=%async_computation.1 | async-start | bytes 2097152 | tf_op jit(solution)/shard_map/all_to_all | solution.py:141
  160.5 87.6 %reduce-scatter.2.cloned.1.call-done = bf16[32,4224]{1,0:T(8,128)(2,1)} async-done(((bf16[1024,4224]{1,0:T(8,128)(2,1)}), bf16[32,4224]{1,0:T(8,128)(2,1)}) %reduce-scatter.2.cloned.1.call-update) | async-done | bytes 270352 | tf_op jit(solution)/shard_map/reduce_scatter | solution.py:160
  250.8 72.4 %all-reduce.2.cloned.1.call-done = bf16[32,4224]{1,0:T(8,128)(2,1)} async-done(((bf16[32,4224]{1,0:T(8,128)(2,1)}), bf16[32,4224]{1,0:T(8,128)(2,1)}) %all-reduce.2.cloned.1.call-update) | async-done | bytes 270352 | tf_op jit(solution)/shard_map/psum | solution.py:161
  (96 shorter events, 41.4 us)
Async XLA Ops:
  7.2 17.1 %copy-start = (bf16[1,8,64,1024]{3,2,1,0:T(8,128)(2,1)S(1)}, bf16[1,8,64,1024]{3,2,1,0:T(8,128)(2,1)}, u32[]{:S(2)}) copy-start(bf16[1,8,64,1024]{3,2,1,0:T(8,128)(2,1)} %param.12) | copy-start | bytes 3145732
  7.2 6.3 %copy-start.1 = (bf16[1,128,1024]{2,1,0:T(8,128)(2,1)S(1)}, bf16[1,128,1024]{2,1,0:T(8,128)(2,1)}, u32[]{:S(2)}) copy-start(bf16[1,128,1024]{2,1,0:T(8,128)(2,1)} %param.19) | copy-start | bytes 786436
  7.2 65.2 %all-gather.2.cloned.1.call-start = ((), (), s32[]{:S(2)}) async-start(), calls=%async_computation.3 | async-start | bytes 8921088 | tf_op jit(solution)/shard_map/all_gather | solution.py:100
  14.6 9.6 %copy-start.7 = (s32[1,8,64]{2,1,0:T(8,128)S(1)}, s32[1,8,64]{2,1,0:T(8,128)}, u32[]{:S(2)}) copy-start(s32[1,8,64]{2,1,0:T(8,128)} %param.13) | copy-start | bytes 6148
  15.7 26.0 %all-to-all-start = ((bf16[8,32,1024]{2,1,0:T(8,128)(2,1)}), bf16[8,32,1024]{2,1,0:T(8,128)(2,1)S(1)}, u32[]{:S(2)}, u32[]{:S(2)}) async-start(bf16[8,32,1024]{2,1,0:T(8,128)(2,1)} %select_select_fusion), calls=%async_computation | async-start | bytes 1048576 | tf_op jit(solution)/shard_map/all_to_all | solution.py:134
  24.2 223.9 %reduce-scatter.2.cloned.1.call-start = ((), (), s32[]{:S(2)}) async-start(), calls=%async_computation.4 | async-start | bytes 8921088 | tf_op jit(solution)/shard_map/reduce_scatter | solution.py:160
  110.6 3.2 copy-start.2
  110.6 3.2 copy-start.8
  113.8 1.6 copy-start.6
  132.6 3.6 %copy-start.4 = (bf16[256,1024]{1,0:T(8,128)(2,1)S(1)}, bf16[256,1024]{1,0:T(8,128)(2,1)}, u32[]{:S(2)}) copy-start(bf16[256,1024]{1,0:T(8,128)(2,1)} %reshape.305) | copy-start | bytes 1572868
  132.6 3.6 %copy-start.5 = (bf16[8,32,1024]{2,1,0:T(8,128)(2,1)S(1)}, bf16[8,32,1024]{2,1,0:T(8,128)(2,1)}, u32[]{:S(2)}) copy-start(bf16[8,32,1024]{2,1,0:T(8,128)(2,1)} %broadcast_select_fusion.1) | copy-start | bytes 1572868
  136.1 1.4 copy-start.3
  153.4 94.7 %all-to-all-start.1 = ((bf16[8,32,2048]{2,1,0:T(8,128)(2,1)}), bf16[8,32,2048]{2,1,0:T(8,128)(2,1)S(1)}, u32[]{:S(2)}, u32[]{:S(2)}) async-start(bf16[8,32,2048]{2,1,0:T(8,128)(2,1)} %broadcast_select_fusion), calls=%async_computation.1 | async-start | bytes 2097152 | tf_op jit(solution)/shard_map/all_to_all | solution.py:141
  160.4 162.8 %all-reduce.2.cloned.1.call-start = ((), (), s32[]{:S(2)}) async-start(), calls=%async_computation.5 | async-start | bytes 540672 | tf_op jit(solution)/shard_map/psum | solution.py:161
Sparse Core Ops, SparseCore 0:
  11.1 61.2 all-gather.1
  147.3 100.6 reduce-scatter.1
  250.4 72.8 all-reduce.1
where the time goes:
time: 336 us; the launch traced here: 335 us
  waiting for transfers between devices  203 us (60%)
  matrix products  44 us (13%)
  local copies, waits for them, and re-layouts  41.1 us (12%)
  other arithmetic  17.3 us (5%)
  starting transfers between devices  15.6 us (5%)
  between operations  14.1 us (4%)
    reduce_scatter x1, waiting for transfers between devices, on_device(): lax.psum_scatter(partial, 'replica', scatter_dimension=0, tiled=True)  87.6 us
    psum x1, waiting for transfers between devices, on_device(): summed = lax.psum(summed, 'batch').astype(jnp.float32)  72.4 us
    all_gather x1, waiting for transfers between devices, on_device(): lax.all_gather(jnp.concatenate([qkv_weight, out_weight, gain_block], axis...  29.1 us
    all_to_all x1, waiting for transfers between devices, on_device(): lax.all_to_all(backward_rows, 'batch', split_axis=0, concat_axis=0, tiled...  13.4 us
    all_to_all x1, starting transfers between devices, on_device(): lax.all_to_all(backward_rows, 'batch', split_axis=0, concat_axis=0, tiled...  8.47 us
    all_to_all x1, starting transfers between devices, on_device(): lax.all_to_all(jnp.take(jnp.concatenate([result, d_tokens], axis=-1), to_...  7.02 us
  transfers between devices with their start and end apart: 5, of which 4 were waited for; matrix products, arithmetic and copies ran while one was open for 6% of the time, Pallas kernels for 0%

commit v1 on v0

--- a/solution.py
+++ b/solution.py
@@ -158,7 +158,7 @@
         axis=1,
     )
     summed = lax.psum_scatter(partial, "replica", scatter_dimension=0, tiled=True)
-    summed = lax.psum(summed, "batch").astype(jnp.float32)
+    summed = jnp.sum(lax.all_gather(summed, "batch"), axis=0).astype(jnp.float32)
     grad_q = summed[:, :qkv_cols]
     grad_o = summed[:, qkv_cols : qkv_cols + out_cols]
     grad_g = summed[:, qkv_cols + out_cols]

time: 336 us -> 308 us (0.917)
  waiting for transfers between devices: 203 us -> 151 us
  blocking collectives: 0 us -> 44.4 us
  local copies, waits for them, and re-layouts: 41.1 us -> 31 us
  starting transfers between devices: 15.6 us -> 8.58 us
    psum x1 -> x0, waiting for transfers between devices: 72.4 us -> none  [on_device(): summed = lax.psum(summed, 'batch').astype(jnp.float32)]
    all_to_all x0 -> x1, blocking collectives: none -> 44.4 us  [on_device(): lax.all_to_all(jnp.take(jnp.concatenate([result, d_tokens], axis=-1), to_...]
    reduce_scatter x1, waiting for transfers between devices: 87.6 us -> 101 us  [on_device(): lax.psum_scatter(partial, 'replica', scatter_dimension=0, tiled=True)]
    all_gather x0 -> x1, waiting for transfers between devices: none -> 7.46 us  [on_device(): lax.all_gather(summed, 'batch')]
    all_to_all x1 -> x0, starting transfers between devices: 7.02 us -> none  [on_device(): lax.all_to_all(jnp.take(jnp.concatenate([result, d_tokens], axis=-1), to_...]
  transfers between devices with their start and end apart: 5 -> 4, of which waited for: 4 -> 4; matrix products, arithmetic and copies ran while one was open for 6% -> 6% of each run, Pallas kernels for 0% -> 0%
where the time goes in v1:
time: 308 us; the launch traced here: 307 us
  waiting for transfers between devices  151 us (49%)
  blocking collectives  44.4 us (14%)
  matrix products  42.3 us (14%)
  local copies, waits for them, and re-layouts  31 us (10%)
  other arithmetic  16.2 us (5%)
  between operations  14.1 us (5%)
  starting transfers between devices  8.58 us (3%)
    reduce_scatter x1, waiting for transfers between devices, on_device(): lax.psum_scatter(partial, 'replica', scatter_dimension=0, tiled=True)  101 us
    all_to_all x1, blocking collectives, on_device(): lax.all_to_all(jnp.take(jnp.concatenate([result, d_tokens], axis=-1), to_...  44.4 us
    all_gather x1, waiting for transfers between devices, on_device(): lax.all_gather(jnp.concatenate([qkv_weight, out_weight, gain_block], axis...  29.1 us
    all_to_all x1, waiting for transfers between devices, on_device(): lax.all_to_all(backward_rows, 'batch', split_axis=0, concat_axis=0, tiled...  13.4 us
    all_to_all x1, starting transfers between devices, on_device(): lax.all_to_all(backward_rows, 'batch', split_axis=0, concat_axis=0, tiled...  8.47 us
    all_gather x1, waiting for transfers between devices, on_device(): lax.all_gather(summed, 'batch')  7.46 us
  transfers between devices with their start and end apart: 4, of which 4 were waited for; matrix products, arithmetic and copies ran while one was open for 6% of the time, Pallas kernels for 0%

profile of v1, /device:TPU:2, one launch (start us, length us, event | category | flops | bytes accessed | tf_op | source)
XLA Modules:
  0.0 307.1 jit_solution(5081303758662866374)
XLA Ops:
  8.1 1.7 pad_maximum_fusion.2
  15.7 8.5 %all-to-all-start = ((bf16[8,32,1024]{2,1,0:T(8,128)(2,1)}), bf16[8,32,1024]{2,1,0:T(8,128)(2,1)S(1)}, u32[]{:S(2)}, u32[]{:S(2)}) async-start(bf16[8,32,1024]{2,1,0:T(8,128)(2,1)} %select_select_fusion), calls=%async_computation | async-start | bytes 1048576 | tf_op jit(solution)/shard_map/all_to_all | solution.py:134
  24.3 2.8 gather_fusion.3
  28.2 13.4 %all-to-all-done = bf16[8,32,1024]{2,1,0:T(8,128)(2,1)S(1)} async-done(((bf16[8,32,1024]{2,1,0:T(8,128)(2,1)}), bf16[8,32,1024]{2,1,0:T(8,128)(2,1)S(1)}, u32[]{:S(2)}, u32[]{:S(2)}) %all-to-all-start) | async-done | bytes 524320 | tf_op jit(solution)/shard_map/all_to_all | solution.py:134
  43.3 29.1 %all-gather.4.cloned.1.call-done = bf16[1024,4224]{1,0:T(8,128)(2,1)} async-done(((bf16[32,4224]{1,0:T(8,128)(2,1)}), bf16[1024,4224]{1,0:T(8,128)(2,1)}) %all-gather.4.cloned.1.call-update) | async-done | bytes 8650768 | tf_op jit(solution)/shard_map/all_gather | solution.py:100
  72.4 2.3 fusion.43
  76.5 4.7 %fusion.6 = bf16[256,3072]{1,0:T(8,128)(2,1)S(1)} fusion(bf16[1024,4224]{1,0:T(8,128)(2,1)} %all-gather.4.cloned.1.call-done, f32[1024]{0:T(1024)S(1)} %convert_reduce_fusion.1, f32[256]{0:T(256)S(1)} %rsqrt.12, f32[256]{0:T(256)S(1)} %div.51, bf16[256,1024]{1,0:T(8,128)(2,1)S(1)} %gather_fusion.3, pred[256]{0:T(512)(128)(4,1)S(1)} %compare_and_fusion.4), kind=kOutput, calls=%fused_computation.14 | convolution fusion | flops 1612972032 | bytes 8395008 | tf_op jit(solution)/shard_map/dot_general | solution.py:27
  82.2 2.5 reshape.302
  84.7 1.6 reshape.304
  86.4 1.6 reshape.303
  88.0 3.2 %fusion.66 = f32[8,16,32,32]{2,3,1,0:T(8,128)} fusion(bf16[8,32,16,64]{3,2,1,0:T(8,128)(2,1)S(1)} %reshape.307, bf16[8,32,16,64]{3,2,1,0:T(8,128)(2,1)} %reshape.302), kind=kOutput, calls=%fused_computation.65 | convolution fusion | flops 16777216 | bytes 1572864 | tf_op jit(solution)/shard_map/gqhd,gkhd->ghqk/dot_general | solution.py:51
  91.2 4.1 %fusion.111 = (f32[8,16,32]{2,1,0:T(8,128)S(1)}, f32[8,16,32,32]{2,3,1,0:T(8,128)}) fusion(pred[8,32]{1,0:T(8,128)(4,1)S(1)} %iota_compare_fusion.3, bf16[8,32,16,64]{3,2,1,0:T(8,128)(2,1)} %reshape.304, bf16[8,32,16,64]{3,2,1,0:T(8,128)(2,1)} %reshape.303), kind=kOutput, calls=%fused_computation.155 | convolution fusion | flops 17301536 | bytes 1589504 | tf_op jit(solution)/shard_map/sub | solution.py:34
  95.3 5.8 %fusion.34 = bf16[8,32,16,64]{3,1,2,0:T(8,128)(2,1)} fusion(f32[8,16,32,32]{2,3,1,0:T(8,128)} %fusion.66, bf16[8,32,16,64]{3,2,1,0:T(8,128)(2,1)} %reshape.304, f32[8,16,32,32]{2,3,1,0:T(8,128)} %get-tuple-element.37, f32[8,16,32]{2,1,0:T(8,128)S(1)} %get-tuple-element.36), kind=kOutput, calls=%fused_computation.35 | convolution fusion | flops 17960992 | bytes 2113536 | tf_op jit(solution)/shard_map/ghqk,gkhd->gqhd/dot_general | solution.py:55
  101.0 5.6 %fusion.31 = bf16[8,32,16,64]{3,1,2,0:T(8,128)(2,1)} fusion(f32[8,16,32,32]{2,3,1,0:T(8,128)} %fusion.66, bf16[8,32,16,64]{3,2,1,0:T(8,128)(2,1)} %reshape.303, f32[8,16,32,32]{2,3,1,0:T(8,128)} %get-tuple-element.37, f32[8,16,32]{2,1,0:T(8,128)S(1)} %get-tuple-element.36), kind=kOutput, calls=%fused_computation.34 | convolution fusion | flops 17960992 | bytes 2113536 | tf_op jit(solution)/shard_map/ghqk,gqhd->gkhd/dot_general | solution.py:58
  106.7 3.2 %fusion.30 = bf16[8,32,16,64]{3,1,2,0:T(8,128)(2,1)} fusion(bf16[8,32,16,64]{3,2,1,0:T(8,128)(2,1)S(1)} %reshape.307, f32[8,16,32,32]{2,3,1,0:T(8,128)} %get-tuple-element.37, f32[8,16,32]{2,1,0:T(8,128)S(1)} %get-tuple-element.36), kind=kOutput, calls=%fused_computation.33 | convolution fusion | flops 17301504 | bytes 1589248 | tf_op jit(solution)/shard_map/ghqk,gqhd->gkhd/dot_general | solution.py:48
  109.9 1.6 fusion.29
  123.2 3.8 %convolution_convert_fusion = bf16[1024,3072]{1,0:T(8,128)(2,1)S(1)} fusion(bf16[256,3072]{1,0:T(8,128)(2,1)} %constant_dynamic-update-slice_fusion, f32[1024]{0:T(1024)S(1)} %convert_reduce_fusion.1, f32[256]{0:T(256)S(1)} %rsqrt.12, f32[256]{0:T(256)S(1)} %div.51, bf16[256,1024]{1,0:T(8,128)(2,1)S(1)} %gather_fusion.3, pred[256]{0:T(512)(128)(4,1)S(1)} %compare_and_fusion.4), kind=kOutput, calls=%fused_computation.9 | convolution fusion | flops 1615331328 | bytes 8395008 | tf_op jit(solution)/shard_map/dot_general | solution.py:89
  128.4 4.9 %fusion.57 = (bf16[1024]{0:T(1024)(128)(2,1)S(1)}, f32[256]{0:T(256)S(1)}, f32[256]{0:T(256)S(1)}, f32[256,1024]{1,0:T(8,128)S(1)}) fusion(f32[256]{0:T(256)S(1)} %rsqrt.12, f32[256]{0:T(256)S(1)} %div.51, bf16[256,1024]{1,0:T(8,128)(2,1)S(1)} %gather_fusion.3, pred[256]{0:T(512)(128)(4,1)S(1)} %compare_and_fusion.4, f32[1024]{0:T(1024)S(1)} %convert_reduce_fusion.1, ...), kind=kOutput, calls=%fused_computation.53 | convolution fusion | flops 1613232640 | bytes 9447680 | tf_op jit(solution)/shard_map/dot_general | solution.py:65
  133.5 3.7 %pad_maximum_fusion = bf16[1024,4224]{1,0:T(8,128)(2,1)} fusion(bf16[1024,128]{1,0:T(8,128)(2,1)S(1)} %broadcast_in_dim.181, bf16[1024,1024]{1,0:T(8,128)(2,1)S(1)} %convolution_convert_fusion.1, bf16[1024,3072]{1,0:T(8,128)(2,1)S(1)} %convolution_convert_fusion), kind=kLoop, calls=%fused_computation.8 | loop fusion | flops 25952256 | bytes 17301504 | tf_op jit(solution)/shard_map/concatenate | solution.py:152
  137.5 100.6 %reduce-scatter.2.cloned.1.call-done = bf16[32,4224]{1,0:T(8,128)(2,1)} async-done(((bf16[1024,4224]{1,0:T(8,128)(2,1)}), bf16[32,4224]{1,0:T(8,128)(2,1)}) %reduce-scatter.2.cloned.1.call-update) | async-done | bytes 270352 | tf_op jit(solution)/shard_map/reduce_scatter | solution.py:160
  238.6 2.3 fusion.40
  241.8 44.4 %all_to_all.10 = bf16[8,32,2048]{2,1,0:T(8,128)(2,1)S(1)} all-to-all(bf16[8,32,2048]{2,1,0:T(8,128)(2,1)S(1)} %broadcast_select_fusion), channel_id=1, replica_groups=mesh['batch'=8,'replica'=32] {'batch'}, dimensions={0} | all-to-all | bytes 2097152 | tf_op jit(solution)/shard_map/all_to_all | solution.py:141
  288.9 7.5 %all-gather.6.cloned.1.call-done = bf16[256,4224]{1,0:T(8,128)(2,1)} async-done(((bf16[32,4224]{1,0:T(8,128)(2,1)}), bf16[256,4224]{1,0:T(8,128)(2,1)}) %all-gather.6.cloned.1.call-update) | async-done | bytes 2162704 | tf_op jit(solution)/shard_map/all_gather | solution.py:161
  296.4 2.0 reduce_sum.135
  (98 shorter events, 32.0 us)
Async XLA Ops:
  7.2 17.1 %copy-start = (bf16[1,8,64,1024]{3,2,1,0:T(8,128)(2,1)S(1)}, bf16[1,8,64,1024]{3,2,1,0:T(8,128)(2,1)}, u32[]{:S(2)}) copy-start(bf16[1,8,64,1024]{3,2,1,0:T(8,128)(2,1)} %param.12) | copy-start | bytes 3145732
  7.2 6.3 %copy-start.2 = (bf16[1,128,1024]{2,1,0:T(8,128)(2,1)S(1)}, bf16[1,128,1024]{2,1,0:T(8,128)(2,1)}, u32[]{:S(2)}) copy-start(bf16[1,128,1024]{2,1,0:T(8,128)(2,1)} %param.19) | copy-start | bytes 786436
  7.2 65.2 %all-gather.4.cloned.1.call-start = ((), (), s32[]{:S(2)}) async-start(), calls=%async_computation.3 | async-start | bytes 8921088 | tf_op jit(solution)/shard_map/all_gather | solution.py:100
  14.6 9.6 %copy-start.8 = (s32[1,8,64]{2,1,0:T(8,128)S(1)}, s32[1,8,64]{2,1,0:T(8,128)}, u32[]{:S(2)}) copy-start(s32[1,8,64]{2,1,0:T(8,128)} %param.13) | copy-start | bytes 6148
  15.7 26.0 %all-to-all-start = ((bf16[8,32,1024]{2,1,0:T(8,128)(2,1)}), bf16[8,32,1024]{2,1,0:T(8,128)(2,1)S(1)}, u32[]{:S(2)}, u32[]{:S(2)}) async-start(bf16[8,32,1024]{2,1,0:T(8,128)(2,1)} %select_select_fusion), calls=%async_computation | async-start | bytes 1048576 | tf_op jit(solution)/shard_map/all_to_all | solution.py:134
  24.2 213.9 %reduce-scatter.2.cloned.1.call-start = ((), (), s32[]{:S(2)}) async-start(), calls=%async_computation.4 | async-start | bytes 8921088 | tf_op jit(solution)/shard_map/reduce_scatter | solution.py:160
  106.7 3.2 %copy-start.3 = (bf16[8,32,16,64]{3,2,1,0:T(8,128)(2,1)S(1)}, bf16[8,32,16,64]{3,2,1,0:T(8,128)(2,1)}, u32[]{:S(2)}) copy-start(bf16[8,32,16,64]{3,2,1,0:T(8,128)(2,1)} %reshape.302) | copy-start | bytes 1572868
  106.7 3.2 %copy-start.9 = (f32[8,16,32,32]{2,3,1,0:T(8,128)S(1)}, f32[8,16,32,32]{2,3,1,0:T(8,128)}, u32[]{:S(2)}) copy-start(f32[8,16,32,32]{2,3,1,0:T(8,128)} %get-tuple-element.37) | copy-start | bytes 1572868
  109.9 1.6 copy-start.7
  123.2 3.8 %copy-start.5 = (bf16[256,1024]{1,0:T(8,128)(2,1)S(1)}, bf16[256,1024]{1,0:T(8,128)(2,1)}, u32[]{:S(2)}) copy-start(bf16[256,1024]{1,0:T(8,128)(2,1)} %reshape.305) | copy-start | bytes 1572868
  123.2 3.8 %copy-start.6 = (bf16[8,32,1024]{2,1,0:T(8,128)(2,1)S(1)}, bf16[8,32,1024]{2,1,0:T(8,128)(2,1)}, u32[]{:S(2)}) copy-start(bf16[8,32,1024]{2,1,0:T(8,128)(2,1)} %broadcast_select_fusion.1) | copy-start | bytes 1572868
  126.9 1.4 copy-start.4
  137.2 159.2 %all-gather.6.cloned.1.call-start = ((), (), s32[]{:S(2)}) async-start(), calls=%async_computation.5 | async-start | bytes 2433024 | tf_op jit(solution)/shard_map/all_gather | solution.py:161
  296.4 4.1 %copy-start.1 = (bf16[1,8,64,1024]{3,2,1,0:T(8,128)(2,1)S(1)}, bf16[1,8,64,1024]{3,2,1,0:T(8,128)(2,1)}, u32[]{:S(2)}) copy-start(bf16[1,8,64,1024]{3,2,1,0:T(8,128)(2,1)} %param.12) | copy-start | bytes 3145732
Sparse Core Ops, SparseCore 0:
  11.1 61.2 all-gather.3
  137.3 100.7 reduce-scatter.1
  239.9 56.4 all-gather.5
